TPU v7x, 32 devices: a whole 2x2x4 slice. The times are simulated.
32 devices in a mesh: cells: 8 (over z, y), slab: 4 (over x, core).
Axes of the slice: x: 2, y: 2, z: 4, core: 2. Of those that a mesh axis runs over, the one named last changes fastest.
Arguments:
- grad: float32 [2, 2, 64, 8192], P(None, None, 'slab', 'cells'), may hold values from -6 to 6
- acc_block: float32 [2, 4, 64, 8192], P(None, None, 'slab', 'cells')
- mobility: float32 [2, 2, 64, 8192], P(None, None, 'slab', 'cells'), may hold values from 0.2 to 1.5
- store: float32 [2, 2, 64, 8192], P(None, None, 'slab', 'cells'), may hold values from 0.1 to 0.5
- trans_h: float32 [64, 8192], P('slab', 'cells'), may hold values from 0.3 to 3
- trans_v: float32 [64, 8192], P('slab', 'cells'), may hold values from 0.3 to 3
- fault_near: int32 [4, 16384], P('slab', 'cells'), may hold values from 0 to 16383
- fault_far: int32 [4, 16384], P('slab', 'cells'), may hold values from 0 to 16383
- fault_trans: float32 [4, 16384], P('slab', 'cells'), may hold values from 0.3 to 3
- fault_count: int32 [4, 8], P('slab', 'cells'), may hold values from 256 to 2048, as said below
- compl_cell: int32 [4, 1024], P('slab', 'cells'), may hold values from 0 to 16383
- compl_well: int32 [4, 1024], P('slab', 'cells'), may hold values from 0 to 15, as said below
- compl_wi: float32 [4, 1024], P('slab', 'cells'), may hold values from 0.5 to 5
Outputs:
- adjoint: float32 [2, 2, 64, 8192], P(None, None, 'slab', 'cells')
- res_history: float32 [2, 2], replicated
Inputs may be any that keep to these rules, and one draw needn't show every extreme that they name: `fault_count`: slots past a pair's count are padding; in every draw some pair of column blocks c, c+1 with c < 7 holds exactly 2048 live slots; the count of the last column block is unused. `compl_well`: every well of a group has at least one completion on the group's device of slab 0.
All inputs are finite; a program needn't handle non-finite values.
Results may differ from a plain program's by a relative error of at most 0.0001.
Values sent between devices are 32-bit elements; how exact they have to be, the bound alone decides.
No kernel may reach another device: no remote copies, remote signals or barrier semaphores. Data moves between devices by JAX's collectives and lax.ppermute only.
A program may use at most 128 MiB of HBM per device.

v0:
```python
import jax
import jax.numpy as jnp
from jax import lax
from jax.sharding import PartitionSpec as P

WELLS = 16
NSTEPS = 2


def shifted(value, axis, by):
    length = lax.axis_size(axis)
    pairs = [(i, i + by) for i in range(length) if 0 <= i + by < length]
    return lax.ppermute(value, axis, pairs)


def extended(block, sides, width):
    for axis, dim in sides:
        count = lax.axis_size(axis)
        forward = [(i, i + 1) for i in range(count - 1)]
        backward = [(target, source) for source, target in forward]
        low = lax.ppermute(
            lax.slice_in_dim(block, block.shape[dim] - width, None, axis=dim), axis, forward
        )
        high = lax.ppermute(lax.slice_in_dim(block, 0, width, axis=dim), axis, backward)
        block = jnp.concatenate([low, block, high], axis=dim)
    return block


def squares(residual):
    return lax.psum(jnp.sum(residual * residual), ("cells", "slab"))


def per_device(
    grad,
    acc_block,
    mobility,
    store,
    trans_h,
    trans_v,
    fault_near,
    fault_far,
    fault_trans,
    fault_count,
    compl_cell,
    compl_well,
    compl_wi,
):
    highest = lax.Precision.HIGHEST
    layer_count, column_count = trans_h.shape
    cells_size = lax.axis_size("cells")
    slab_size = lax.axis_size("slab")
    cells_place = lax.axis_index("cells")
    slab_place = lax.axis_index("slab")
    column_ids = lax.broadcasted_iota(jnp.int32, (layer_count, column_count), 1)
    layer_ids = lax.broadcasted_iota(jnp.int32, (layer_count, column_count), 0)
    zero_value = jnp.zeros((), trans_h.dtype)
    trans_east = jnp.where(
        (cells_place == cells_size - 1) & (column_ids == column_count - 1), zero_value, trans_h
    )
    trans_down = jnp.where(
        (slab_place == slab_size - 1) & (layer_ids == layer_count - 1), zero_value, trans_v
    )
    east_edge = shifted(trans_east[:, -1], "cells", 1)
    down_edge = shifted(trans_down[-1, :], "slab", 1)
    trans_west = jnp.concatenate([east_edge[:, None], trans_east[:, :-1]], axis=1)
    trans_up = jnp.concatenate([down_edge[None, :], trans_down[:-1, :]], axis=0)
    face_total = trans_east + trans_west + trans_down + trans_up
    near_cells = fault_near.reshape(-1)
    far_cells = fault_far.reshape(-1)
    slot_count = near_cells.shape[0]
    slot_live = (jnp.arange(slot_count, dtype=jnp.int32) < fault_count.reshape(())) & (
        cells_place < cells_size - 1
    )
    weight_here = jnp.where(slot_live, fault_trans.reshape(-1), zero_value)
    weight_left = shifted(weight_here, "cells", 1)
    well_cells = compl_cell.reshape(-1)
    well_index = compl_wi.reshape(-1)
    well_onehot = (
        compl_well.reshape(-1)[:, None] == jnp.arange(WELLS, dtype=jnp.int32)[None, :]
    ).astype(trans_h.dtype)
    well_totals = lax.psum(jnp.dot(well_index, well_onehot, precision=highest), "slab")
    solutions = [None] * NSTEPS
    histories = [None] * NSTEPS
    adjoint_next = jnp.zeros(grad.shape[1:], grad.dtype)
    for newton in range(NSTEPS - 1, -1, -1):
        block = acc_block[newton]
        mobile = mobility[newton]
        diag_first = block[0] + mobile[0] * face_total
        diag_second = block[3] + mobile[1] * face_total
        determinant = diag_first * diag_second - block[1] * block[2]
        inverse_aa = diag_second / determinant
        inverse_ab = -block[1] / determinant
        inverse_ba = -block[2] / determinant
        inverse_bb = diag_first / determinant
        residual = grad[newton] + store[newton] * adjoint_next
        history = []
        norm_square = squares(residual)
        precond = jnp.stack(
            [
                inverse_aa * residual[0] + inverse_ab * residual[1],
                inverse_ba * residual[0] + inverse_bb * residual[1],
            ]
        )
        scaled = mobile * precond
        flat = scaled.reshape(2, -1)
        picks_near = flat[:, near_cells]
        picks_far = flat[:, far_cells]
        padded = extended(scaled, (("cells", 2), ("slab", 1)), 1)
        east = padded[:, 1:-1, 2:]
        west = padded[:, 1:-1, :-2]
        below = padded[:, 2:, 1:-1]
        above = padded[:, :-2, 1:-1]
        from_left = shifted(picks_near, "cells", 1)
        from_right = shifted(picks_far, "cells", -1)
        laplace = (
            trans_east * (scaled - east)
            + trans_west * (scaled - west)
            + trans_down * (scaled - below)
            + trans_up * (scaled - above)
        )
        flux_right = weight_here * (picks_near - from_right)
        flux_left = weight_left * (from_left - picks_far)
        fault_term = (
            jnp.zeros_like(flat).at[:, near_cells].add(flux_right).at[:, far_cells].add(-flux_left)
        )
        fault_term = fault_term.reshape(2, layer_count, column_count)
        pressure = precond[0].reshape(-1)
        values = pressure[well_cells]
        rates = lax.psum(jnp.dot(well_index * values, well_onehot, precision=highest), "slab")
        back = jnp.dot(well_onehot, rates / well_totals, precision=highest)
        well_term = (
            jnp.zeros_like(pressure)
            .at[well_cells]
            .add(well_index * (values - back))
            .reshape(layer_count, column_count)
        )
        first = (
            block[0] * precond[0] + block[1] * precond[1] + laplace[0] + fault_term[0] + well_term
        )
        second = block[2] * precond[0] + block[3] * precond[1] + laplace[1] + fault_term[1]
        image = jnp.stack([first, second])
        along, energy = lax.psum(
            (jnp.sum(residual * image), jnp.sum(image * image)), ("cells", "slab")
        )
        history.append(jnp.sqrt(norm_square))
        alpha = along / energy
        solution = alpha * precond
        residual = residual - alpha * image
        closing = squares(residual)
        history.append(jnp.sqrt(closing))
        solutions[newton] = solution
        histories[newton] = jnp.stack(history)
        adjoint_next = solution
    return (jnp.stack(solutions), jnp.stack(histories))


def solution(mesh):
    placed = (
        P(None, None, "slab", "cells"),
        P(None, None, "slab", "cells"),
        P(None, None, "slab", "cells"),
        P(None, None, "slab", "cells"),
        P("slab", "cells"),
        P("slab", "cells"),
        P("slab", "cells"),
        P("slab", "cells"),
        P("slab", "cells"),
        P("slab", "cells"),
        P("slab", "cells"),
        P("slab", "cells"),
        P("slab", "cells"),
    )
    return jax.shard_map(
        per_device,
        mesh=mesh,
        in_specs=placed,
        out_specs=(P(None, None, "slab", "cells"), P()),
        check_vma=False,
    )
```

profile of v0, /device:TPU:0, one launch (start us, length us, event | category | flops | bytes accessed | tf_op | source)
XLA Modules:
  0.0 379.6 jit_solution(11750703015133822277)
XLA Ops:
  0.6 0.9 broadcast_select_fusion.1
  1.7 4.9 %collective-permute-start = (f32[16]{0:T(128)S(1)}, f32[16]{0:T(128)S(1)}, u32[]{:S(2)}, u32[]{:S(2)}) collective-permute-start(f32[16]{0:T(128)S(1)} %slice_reduce_fusion.4), channel_id=1, source_target_pairs={{0,4},{4,8},{8,12},{12,16},{16,20},{20,24},{24,28},{1,5},{5,9},{9,... | collective-permute-start | bytes 200 | tf_op jit(solution)/shard_map/ppermute | solution.py:13
  6.6 0.9 broadcast_select_fusion
  7.5 1.5 collective-permute-start.1
  9.6 0.7 fusion.81
  10.3 3.4 collective-permute-start.7
  13.8 1.0 fusion.91
  14.7 0.7 compare_select_fusion
  15.5 0.7 compare_select_fusion.1
  16.2 0.7 and_select_fusion
  16.9 0.7 fusion.83
  17.6 1.0 multiply_add_fusion
  18.6 0.9 convolution_bitcast_fusion.3
  19.6 4.6 %copy.39 = f32[1,2,16,1024]{1,3,2,0:T(8,128)} copy(f32[1,2,16,1024]{3,2,1,0:T(8,128)S(1)} %get-tuple-element.35) | data formatting | bytes 262144 | tf_op jit(solution)/shard_map/slice | solution.py:87
  24.2 4.7 %copy.45 = f32[1,2,16,1024]{1,3,2,0:T(8,128)} copy(f32[1,2,16,1024]{3,2,1,0:T(8,128)S(1)} %get-tuple-element.34) | data formatting | bytes 262144 | tf_op jit(solution)/shard_map/slice | solution.py:87
  29.4 5.0 %copy.40 = f32[2,16384]{0,1:T(8,128)} copy(f32[2,16384]{1,0:T(2,128)S(1)} %pad_maximum_fusion.10) | data formatting | bytes 262144 | tf_op jit(solution)/shard_map/stack | solution.py:98
  34.4 9.8 %bitcast_multiply_fusion.1 = f32[2,16384]{0,1:T(8,128)} fusion(f32[2,16384]{0,1:T(8,128)} %copy.40, f32[1,2,16,1024]{1,3,2,0:T(8,128)} %copy.39), kind=kLoop, calls=%fused_computation.17 | loop fusion | flops 32768 | bytes 393216 | tf_op jit(solution)/shard_map/mul | solution.py:104
  44.2 8.8 %gather_fusion.1 = f32[2048,2]{1,0:T(8,128)S(1)} fusion(f32[2,16384]{0,1:T(8,128)} %bitcast_multiply_fusion.1, s32[2048]{0:T(1024)S(1)} %broadcast_clamp_fusion), kind=kCustom, calls=%fused_computation.1 | custom fusion | bytes 40960 | tf_op jit(solution)/shard_map/gather | solution.py:107
  53.4 1.3 collective-permute-start.6
  54.7 8.8 %gather_fusion = f32[2048,2]{1,0:T(8,128)S(1)} fusion(f32[2,16384]{0,1:T(8,128)} %bitcast_multiply_fusion.1, s32[2048]{0:T(1024)S(1)} %broadcast_clamp_fusion.1), kind=kCustom, calls=%fused_computation | custom fusion | bytes 40960 | tf_op jit(solution)/shard_map/gather | solution.py:106
  63.9 4.5 %collective-permute-start.8 = (f32[2,2048]{1,0:T(2,128)S(1)}, f32[2,2048]{1,0:T(2,128)S(1)}, u32[]{:S(2)}, u32[]{:S(2)}) collective-permute-start(f32[2,2048]{1,0:T(2,128)S(1)} %bitcast.381), channel_id=1, source_target_pairs={{0,4},{4,8},{8,12},{12,16},{16,20},{20,24},{24,28},{1,5},{5,9},{9,... | collective-permute-start | bytes 49160 | tf_op jit(solution)/shard_map/ppermute | solution.py:13
  68.5 1.3 collective-permute-start.2
  69.8 5.0 %collective-permute-start.3 = (f32[2,16,1]{2,1,0:T(8,128)S(1)}, f32[2,16,1]{2,1,0:T(8,128)S(1)}, u32[]{:S(2)}, u32[]{:S(2)}) collective-permute-start(f32[2,16,1]{2,1,0:T(8,128)S(1)} %get-tuple-element.43), channel_id=1, source_target_pairs={{0,4},{4,8},{8,12},{12,16},{16,20},{20,24},{24,28},{1,5},{5,9},{9,... | collective-permute-start | bytes 392 | tf_op jit(solution)/shard_map/ppermute | solution.py:21
  74.8 1.1 gather_fusion.2
  76.2 6.6 %all-reduce.3 = (f32[16]{0:T(128)S(1)}, f32[16]{0:T(128)S(1)}) all-reduce(f32[16]{0:T(128)S(1)} %convolution_bitcast_fusion.4, f32[16]{0:T(128)S(1)} %convolution_bitcast_fusion.3), channel_id=1, replica_groups=mesh['cells'=8,'slab'=4] {'slab'}, use_global_device_ids=true, to_apply=%region_2.3 | all-reduce | flops 32 | bytes 256 | tf_op jit(solution)/shard_map/psum | solution.py:129
  82.9 1.3 collective-permute-start.4
  84.2 3.0 collective-permute-start.5
  87.5 1.3 scatter_custom_fusion.2
  89.2 0.4 copy.43
  89.6 15.2 %scatter_custom_fusion = f32[2,16384]{0,1:T(8,128)} fusion(s32[2048]{0:T(1024)S(1)} %bitcast.386, f32[2048,2]{1,0:T(8,128)S(1)} %copy.43, f32[]{:T(128)} %constant.10.clone.1), kind=kCustom, calls=%fused_computation.20 | custom fusion | flops 4096 | bytes 131076 | tf_op jit(solution)/shard_map/scatter-add | solution.py:124
  104.8 0.4 copy.44
  105.1 16.9 %scatter_fusion = f32[2,16384]{0,1:T(8,128)} fusion(f32[2,16384]{0,1:T(8,128)} %scatter_custom_fusion, s32[2048]{0:T(1024)S(1)} %bitcast.376, f32[2048,2]{1,0:T(8,128)S(1)} %copy.44), kind=kCustom, calls=%fused_computation.7 | custom fusion | flops 4096 | bytes 57344 | tf_op jit(solution)/shard_map/scatter-add | solution.py:124
  122.0 12.5 %slice_reduce_fusion.3 = (f32[16384]{0:T(1024)S(1)}, f32[16384]{0:T(1024)S(1)}) fusion(f32[2,16384]{0,1:T(8,128)} %scatter_fusion), kind=kLoop, calls=%fused_computation.15 | loop fusion | bytes 262144 | tf_op jit(solution)/shard_map/slice | solution.py:138
  134.7 0.7 multiply_reduce_fusion.4
  135.3 42.9 %all-reduce.2 = (f32[]{:T(128)}, f32[]{:T(128)}) all-reduce(f32[]{:T(128)} %get-tuple-element.13, f32[]{:T(128)} %get-tuple-element.12), channel_id=1, replica_groups=mesh['cells'=8,'slab'=4] {'cells','slab'}, use_global_device_ids=true, to_apply=%region_6.7 | all-reduce | flops 2 | bytes 16 | tf_op jit(solution)/shard_map/psum | solution.py:142
  180.0 5.0 %copy.46 = f32[2,16384]{0,1:T(8,128)} copy(f32[2,16384]{1,0:T(2,128)S(1)} %pad_maximum_fusion.12) | data formatting | bytes 262144 | tf_op jit(solution)/shard_map/stack | solution.py:98
  185.0 9.8 %bitcast_multiply_fusion = f32[2,16384]{0,1:T(8,128)} fusion(f32[2,16384]{0,1:T(8,128)} %copy.46, f32[1,2,16,1024]{1,3,2,0:T(8,128)} %copy.45), kind=kLoop, calls=%fused_computation.16 | loop fusion | flops 32768 | bytes 393216 | tf_op jit(solution)/shard_map/mul | solution.py:104
  194.7 8.8 %gather_fusion.3 = f32[2048,2]{1,0:T(8,128)S(1)} fusion(f32[2,16384]{0,1:T(8,128)} %bitcast_multiply_fusion, s32[2048]{0:T(1024)S(1)} %copy-done.13), kind=kCustom, calls=%fused_computation.3 | custom fusion | bytes 40960 | tf_op jit(solution)/shard_map/gather | solution.py:106
  203.6 9.8 %gather_fusion.4 = f32[2048,2]{1,0:T(8,128)S(1)} fusion(f32[2,16384]{0,1:T(8,128)} %bitcast_multiply_fusion, s32[2048]{0:T(1024)} %copy-done.11), kind=kCustom, calls=%fused_computation.4 | custom fusion | bytes 40960 | tf_op jit(solution)/shard_map/gather | solution.py:107
  213.4 1.5 fusion.31
  215.0 4.4 %collective-permute-start.10 = (f32[2,16,1]{2,1,0:T(8,128)S(1)}, f32[2,16,1]{2,1,0:T(8,128)S(1)}, u32[]{:S(2)}, u32[]{:S(2)}) collective-permute-start(f32[2,16,1]{2,1,0:T(8,128)S(1)} %get-tuple-element.41), channel_id=1, source_target_pairs={{0,4},{4,8},{8,12},{12,16},{16,20},{20,24},{24,28},{1,5},{5,9},{9,... | collective-permute-start | bytes 392 | tf_op jit(solution)/shard_map/ppermute | solution.py:21
  219.4 1.3 collective-permute-start.9
  221.0 4.5 %collective-permute-start.14 = (f32[2,2048]{1,0:T(2,128)S(1)}, f32[2,2048]{1,0:T(2,128)S(1)}, u32[]{:S(2)}, u32[]{:S(2)}) collective-permute-start(f32[2,2048]{1,0:T(2,128)S(1)} %bitcast.382), channel_id=1, source_target_pairs={{0,4},{4,8},{8,12},{12,16},{16,20},{20,24},{24,28},{1,5},{5,9},{9,... | collective-permute-start | bytes 49160 | tf_op jit(solution)/shard_map/ppermute | solution.py:13
  225.9 1.3 collective-permute-start.13
  227.2 1.3 gather_fusion.5
  228.5 0.9 convolution_bitcast_fusion.1
  229.4 5.8 %psum.81 = f32[16]{0:T(128)S(1)} all-reduce(f32[16]{0:T(128)S(1)} %convolution_bitcast_fusion.1), channel_id=1, replica_groups=mesh['cells'=8,'slab'=4] {'slab'}, use_global_device_ids=true, to_apply=%region_11.12 | all-reduce | flops 16 | bytes 128 | tf_op jit(solution)/shard_map/psum | solution.py:129
  235.3 1.3 collective-permute-start.11
  236.6 3.0 collective-permute-start.12
  239.6 0.9 fusion.7
  240.5 1.5 scatter_custom_fusion.5
  242.0 1.8 fusion.10
  243.8 0.7 negate_bitcast_fusion
  244.5 0.4 copy.50
  245.0 0.4 copy.49
  245.3 15.3 %scatter_custom_fusion.3 = f32[2,16384]{0,1:T(8,128)} fusion(s32[2048]{0:T(1024)} %bitcast.387, f32[2048,2]{1,0:T(8,128)S(1)} %copy.49, f32[]{:T(128)} %constant.10.clone.1), kind=kCustom, calls=%fused_computation.18 | custom fusion | flops 4096 | bytes 131584 | tf_op jit(solution)/shard_map/scatter-add | solution.py:124
  260.6 16.9 %scatter_fusion.1 = f32[2,16384]{0,1:T(8,128)} fusion(f32[2,16384]{0,1:T(8,128)} %scatter_custom_fusion.3, s32[2048]{0:T(1024)S(1)} %bitcast.377, f32[2048,2]{1,0:T(8,128)S(1)} %copy.50), kind=kCustom, calls=%fused_computation.10 | custom fusion | flops 4096 | bytes 57344 | tf_op jit(solution)/shard_map/scatter-add | solution.py:124
  277.5 12.2 %slice_reduce_fusion.1 = (f32[16384]{0:T(1024)S(1)}, f32[16384]{0:T(1024)S(1)}) fusion(f32[2,16384]{0,1:T(8,128)} %scatter_fusion.1), kind=kLoop, calls=%fused_computation.13 | loop fusion | bytes 262144 | tf_op jit(solution)/shard_map/slice | solution.py:138
  289.8 0.6 multiply_reduce_fusion.2
  290.5 41.0 %all-reduce.1 = (f32[]{:T(128)}, f32[]{:T(128)}) all-reduce(f32[]{:T(128)} %get-tuple-element.11, f32[]{:T(128)} %get-tuple-element.10), channel_id=1, replica_groups=mesh['cells'=8,'slab'=4] {'cells','slab'}, use_global_device_ids=true, to_apply=%region_14.15 | all-reduce | flops 2 | bytes 16 | tf_op jit(solution)/shard_map/psum | solution.py:142
  332.8 0.6 multiply_reduce_fusion.1
  333.5 42.0 %all-reduce = (f32[]{:T(128)}, f32[]{:T(128)}, f32[]{:T(128)}, f32[]{:T(128)}) all-reduce(f32[]{:T(128)} %get-tuple-element.9, f32[]{:T(128)} %get-tuple-element.8, f32[]{:T(128)} %get-tuple-element.7, f32[]{:T(128)} %get-tuple-element.6), channel_id=1, replica_groups=mesh['cells'=8,'slab'=4] {'cells','slab'}, use_global_device_ids=true, to_apply=%region_24.25 | all-reduce | flops 4 | bytes 32 | tf_op jit(solution)/shard_map/psum | solution.py:30
  378.3 0.6 pad_maximum_fusion.16
  378.8 0.7 pad_maximum_fusion
  (105 shorter events, 4.0 us)
Async XLA Ops:
  1.7 27.2 %collective-permute-start = (f32[16]{0:T(128)S(1)}, f32[16]{0:T(128)S(1)}, u32[]{:S(2)}, u32[]{:S(2)}) collective-permute-start(f32[16]{0:T(128)S(1)} %slice_reduce_fusion.4), channel_id=1, source_target_pairs={{0,4},{4,8},{8,12},{12,16},{16,20},{20,24},{24,28},{1,5},{5,9},{9,... | collective-permute-start | bytes 200 | tf_op jit(solution)/shard_map/ppermute | solution.py:13
  7.5 81.4 %copy-start.2 = (f32[16,1024]{1,0:T(8,128)}, f32[16,1024]{1,0:T(8,128)S(1)}, u32[]{:S(2)}) copy-start(f32[16,1024]{1,0:T(8,128)S(1)} %broadcast_select_fusion) | copy-start | bytes 196612
  7.5 21.4 %collective-permute-start.1 = (f32[1024]{0:T(1024)S(1)}, f32[1024]{0:T(1024)S(1)}, u32[]{:S(2)}, u32[]{:S(2)}) collective-permute-start(f32[1024]{0:T(1024)S(1)} %bitcast.389), channel_id=1, source_target_pairs={{0,1},{1,2},{2,3},{4,5},{5,6},{6,7},{8,9},{9,10},{10,11},{12,13},{... | collective-permute-start | bytes 12296 | tf_op jit(solution)/shard_map/ppermute | solution.py:13
  10.3 94.4 %collective-permute-start.7 = (f32[2048]{0:T(1024)S(1)}, f32[2048]{0:T(1024)S(1)}, u32[]{:S(2)}, u32[]{:S(2)}) collective-permute-start(f32[2048]{0:T(1024)S(1)} %fusion.81), channel_id=1, source_target_pairs={{0,4},{4,8},{8,12},{12,16},{16,20},{20,24},{24,28},{1,5},{5,9},{9,... | collective-permute-start | bytes 24584 | tf_op jit(solution)/shard_map/ppermute | solution.py:13
  15.5 28.7 %copy-start.11 = (s32[2048]{0:T(1024)}, s32[2048]{0:T(1024)S(1)}, u32[]{:S(2)}) copy-start(s32[2048]{0:T(1024)S(1)} %broadcast_clamp_fusion) | copy-start | bytes 24580
  16.2 73.4 %copy-start.15 = (s32[2048,1]{0,1:T(1,128)}, s32[2048,1]{0,1:T(1,128)S(1)}, u32[]{:S(2)}) copy-start(s32[2048,1]{0,1:T(1,128)S(1)} %compare_select_fusion.1) | copy-start | bytes 24580
  16.2 38.5 %copy-start.12 = (s32[2048]{0:T(1024)}, s32[2048]{0:T(1024)S(1)}, u32[]{:S(2)}) copy-start(s32[2048]{0:T(1024)S(1)} %broadcast_clamp_fusion.1) | copy-start | bytes 24580
  17.6 69.9 %copy-start.17 = (s32[128]{0:T(128)}, s32[128]{0:T(128)S(1)}, u32[]{:S(2)}) copy-start(s32[128]{0:T(128)S(1)} %fusion.83) | copy-start | bytes 1540
  19.5 55.3 %copy-start.16 = (s32[1024]{0:T(1024)}, s32[1024]{0:T(1024)S(1)}, u32[]{:S(2)}) copy-start(s32[1024]{0:T(1024)S(1)} %pad_clamp_fusion) | copy-start | bytes 12292
  19.5 9.4 %copy-start = (f32[2,4,16,1024]{3,2,1,0:T(8,128)S(1)}, f32[2,4,16,1024]{3,2,1,0:T(8,128)}, u32[]{:S(2)}) copy-start(f32[2,4,16,1024]{3,2,1,0:T(8,128)} %param.14) | copy-start | bytes 1572868
  19.5 9.4 %copy-start.1 = (f32[2,2,16,1024]{3,2,1,0:T(8,128)S(1)}, f32[2,2,16,1024]{3,2,1,0:T(8,128)}, u32[]{:S(2)}) copy-start(f32[2,2,16,1024]{3,2,1,0:T(8,128)} %param.15) | copy-start | bytes 786436
  19.5 9.4 %copy-start.9 = (f32[16,1024]{1,0:T(8,128)S(1)}, f32[16,1024]{1,0:T(8,128)}, u32[]{:S(2)}) copy-start(f32[16,1024]{1,0:T(8,128)} %param.17) | copy-start | bytes 196612
  19.5 9.4 %copy-start.10 = (f32[16,1024]{1,0:T(8,128)S(1)}, f32[16,1024]{1,0:T(8,128)}, u32[]{:S(2)}) copy-start(f32[16,1024]{1,0:T(8,128)} %param.18) | copy-start | bytes 196612
  29.1 59.8 %copy-start.3 = (f32[16,1024]{1,0:T(8,128)}, f32[16,1024]{1,0:T(8,128)S(1)}, u32[]{:S(2)}) copy-start(f32[16,1024]{1,0:T(8,128)S(1)} %get-tuple-element.26) | copy-start | bytes 196612
  29.1 59.8 %copy-start.4 = (f32[16,1024]{1,0:T(8,128)}, f32[16,1024]{1,0:T(8,128)S(1)}, u32[]{:S(2)}) copy-start(f32[16,1024]{1,0:T(8,128)S(1)} %get-tuple-element.27) | copy-start | bytes 196612
  34.4 41.6 %copy-start.18 = (s32[1,128]{1,0:T(1,128)S(1)}, s32[1,128]{1,0:T(1,128)}, u32[]{:S(2)}) copy-start(s32[1,128]{1,0:T(1,128)} %param.24) | copy-start | bytes 1540
  34.4 41.6 %copy-start.19 = (f32[1,128]{1,0:T(1,128)S(1)}, f32[1,128]{1,0:T(1,128)}, u32[]{:S(2)}) copy-start(f32[1,128]{1,0:T(1,128)} %param.25) | copy-start | bytes 1540
  53.4 35.8 %collective-permute-start.6 = (f32[2,2048]{1,0:T(2,128)S(1)}, f32[2,2048]{1,0:T(2,128)S(1)}, u32[]{:S(2)}, u32[]{:S(2)}) collective-permute-start(f32[2,2048]{1,0:T(2,128)S(1)} %bitcast.380), channel_id=1, source_target_pairs={{4,0},{8,4},{12,8},{16,12},{20,16},{24,20},{28,24},{5,1},{9,5},{13... | collective-permute-start | bytes 49160 | tf_op jit(solution)/shard_map/ppermute | solution.py:13
  63.9 40.9 %collective-permute-start.8 = (f32[2,2048]{1,0:T(2,128)S(1)}, f32[2,2048]{1,0:T(2,128)S(1)}, u32[]{:S(2)}, u32[]{:S(2)}) collective-permute-start(f32[2,2048]{1,0:T(2,128)S(1)} %bitcast.381), channel_id=1, source_target_pairs={{0,4},{4,8},{8,12},{12,16},{16,20},{20,24},{24,28},{1,5},{5,9},{9,... | collective-permute-start | bytes 49160 | tf_op jit(solution)/shard_map/ppermute | solution.py:13
  68.5 14.3 %collective-permute-start.2 = (f32[2,16,1]{2,1,0:T(8,128)S(1)}, f32[2,16,1]{2,1,0:T(8,128)S(1)}, u32[]{:S(2)}, u32[]{:S(2)}) collective-permute-start(f32[2,16,1]{2,1,0:T(8,128)S(1)} %get-tuple-element.42), channel_id=1, source_target_pairs={{4,0},{8,4},{12,8},{16,12},{20,16},{24,20},{28,24},{5,1},{9,5},{13... | collective-permute-start | bytes 392 | tf_op jit(solution)/shard_map/ppermute | solution.py:24
  69.8 13.0 %collective-permute-start.3 = (f32[2,16,1]{2,1,0:T(8,128)S(1)}, f32[2,16,1]{2,1,0:T(8,128)S(1)}, u32[]{:S(2)}, u32[]{:S(2)}) collective-permute-start(f32[2,16,1]{2,1,0:T(8,128)S(1)} %get-tuple-element.43), channel_id=1, source_target_pairs={{0,4},{4,8},{8,12},{12,16},{16,20},{20,24},{24,28},{1,5},{5,9},{9,... | collective-permute-start | bytes 392 | tf_op jit(solution)/shard_map/ppermute | solution.py:21
  82.8 4.5 %copy-start.20 = (f32[16]{0:T(128)}, f32[16]{0:T(128)S(1)}, u32[]{:S(2)}) copy-start(f32[16]{0:T(128)S(1)} %get-tuple-element.23) | copy-start | bytes 196
  82.9 5.9 %collective-permute-start.4 = (f32[2,1,1026]{2,1,0:T(1,128)S(1)}, f32[2,1,1026]{2,1,0:T(1,128)S(1)}, u32[]{:S(2)}, u32[]{:S(2)}) collective-permute-start(f32[2,1,1026]{2,1,0:T(1,128)S(1)} %get-tuple-element.38), channel_id=1, source_target_pairs={{1,0},{2,1},{3,2},{5,4},{6,5},{7,6},{9,8},{10,9},{11,10},{13,12},{... | collective-permute-start | bytes 24632 | tf_op jit(solution)/shard_map/ppermute | solution.py:24
  84.2 4.6 %collective-permute-start.5 = (f32[2,1,1026]{2,1,0:T(1,128)S(1)}, f32[2,1,1026]{2,1,0:T(1,128)S(1)}, u32[]{:S(2)}, u32[]{:S(2)}) collective-permute-start(f32[2,1,1026]{2,1,0:T(1,128)S(1)} %get-tuple-element.39), channel_id=1, source_target_pairs={{0,1},{1,2},{2,3},{4,5},{5,6},{6,7},{8,9},{9,10},{10,11},{12,13},{... | collective-permute-start | bytes 24632 | tf_op jit(solution)/shard_map/ppermute | solution.py:21
  104.7 29.8 %copy-start.14 = (f32[2048]{0:T(1024)}, f32[2048]{0:T(1024)S(1)}, u32[]{:S(2)}) copy-start(f32[2048]{0:T(1024)S(1)} %collective-permute-done.7) | copy-start | bytes 24580
  122.0 57.5 %copy-start.7 = (f32[2,2,16,1024]{3,2,1,0:T(8,128)S(1)}, f32[2,2,16,1024]{3,2,1,0:T(8,128)}, u32[]{:S(2)}) copy-start(f32[2,2,16,1024]{3,2,1,0:T(8,128)} %param.16) | copy-start | bytes 786436
  122.0 57.5 %copy-start.8 = (f32[2,2,16,1024]{3,2,1,0:T(8,128)S(1)}, f32[2,2,16,1024]{3,2,1,0:T(8,128)}, u32[]{:S(2)}) copy-start(f32[2,2,16,1024]{3,2,1,0:T(8,128)} %param.13) | copy-start | bytes 786436
  134.6 44.9 %copy-start.5 = (f32[1,16,1024]{2,1,0:T(8,128)}, f32[1,16,1024]{2,1,0:T(8,128)S(1)}, u32[]{:S(2)}) copy-start(f32[1,16,1024]{2,1,0:T(8,128)S(1)} %get-tuple-element.33) | copy-start | bytes 196612
  185.0 9.8 %copy-start.13 = (s32[2048]{0:T(1024)S(1)}, s32[2048]{0:T(1024)}, u32[]{:S(2)}) copy-start(s32[2048]{0:T(1024)} %copy-done.12) | copy-start | bytes 24580
  215.0 20.1 %collective-permute-start.10 = (f32[2,16,1]{2,1,0:T(8,128)S(1)}, f32[2,16,1]{2,1,0:T(8,128)S(1)}, u32[]{:S(2)}, u32[]{:S(2)}) collective-permute-start(f32[2,16,1]{2,1,0:T(8,128)S(1)} %get-tuple-element.41), channel_id=1, source_target_pairs={{0,4},{4,8},{8,12},{12,16},{16,20},{20,24},{24,28},{1,5},{5,9},{9,... | collective-permute-start | bytes 392 | tf_op jit(solution)/shard_map/ppermute | solution.py:21
  219.4 15.7 %collective-permute-start.9 = (f32[2,16,1]{2,1,0:T(8,128)S(1)}, f32[2,16,1]{2,1,0:T(8,128)S(1)}, u32[]{:S(2)}, u32[]{:S(2)}) collective-permute-start(f32[2,16,1]{2,1,0:T(8,128)S(1)} %get-tuple-element.40), channel_id=1, source_target_pairs={{4,0},{8,4},{12,8},{16,12},{20,16},{24,20},{28,24},{5,1},{9,5},{13... | collective-permute-start | bytes 392 | tf_op jit(solution)/shard_map/ppermute | solution.py:24
  221.0 22.8 %collective-permute-start.14 = (f32[2,2048]{1,0:T(2,128)S(1)}, f32[2,2048]{1,0:T(2,128)S(1)}, u32[]{:S(2)}, u32[]{:S(2)}) collective-permute-start(f32[2,2048]{1,0:T(2,128)S(1)} %bitcast.382), channel_id=1, source_target_pairs={{0,4},{4,8},{8,12},{12,16},{16,20},{20,24},{24,28},{1,5},{5,9},{9,... | collective-permute-start | bytes 49160 | tf_op jit(solution)/shard_map/ppermute | solution.py:13
  225.9 19.0 %collective-permute-start.13 = (f32[2,2048]{1,0:T(2,128)S(1)}, f32[2,2048]{1,0:T(2,128)S(1)}, u32[]{:S(2)}, u32[]{:S(2)}) collective-permute-start(f32[2,2048]{1,0:T(2,128)S(1)} %bitcast.383), channel_id=1, source_target_pairs={{4,0},{8,4},{12,8},{16,12},{20,16},{24,20},{28,24},{5,1},{9,5},{13... | collective-permute-start | bytes 49160 | tf_op jit(solution)/shard_map/ppermute | solution.py:13
  235.3 6.7 %collective-permute-start.11 = (f32[2,1,1026]{2,1,0:T(1,128)S(1)}, f32[2,1,1026]{2,1,0:T(1,128)S(1)}, u32[]{:S(2)}, u32[]{:S(2)}) collective-permute-start(f32[2,1,1026]{2,1,0:T(1,128)S(1)} %get-tuple-element.36), channel_id=1, source_target_pairs={{1,0},{2,1},{3,2},{5,4},{6,5},{7,6},{9,8},{10,9},{11,10},{13,12},{... | collective-permute-start | bytes 24632 | tf_op jit(solution)/shard_map/ppermute | solution.py:24
  236.6 5.4 %collective-permute-start.12 = (f32[2,1,1026]{2,1,0:T(1,128)S(1)}, f32[2,1,1026]{2,1,0:T(1,128)S(1)}, u32[]{:S(2)}, u32[]{:S(2)}) collective-permute-start(f32[2,1,1026]{2,1,0:T(1,128)S(1)} %get-tuple-element.37), channel_id=1, source_target_pairs={{0,1},{1,2},{2,3},{4,5},{5,6},{6,7},{8,9},{9,10},{10,11},{12,13},{... | collective-permute-start | bytes 24632 | tf_op jit(solution)/shard_map/ppermute | solution.py:21
  277.5 12.3 %copy-start.6 = (f32[2,16,1024]{2,1,0:T(8,128)S(1)}, f32[2,16,1024]{2,1,0:T(8,128)}, u32[]{:S(2)}) copy-start(f32[2,16,1024]{2,1,0:T(8,128)} %fusion.10) | copy-start | bytes 393220
where the time goes:
time: 381 us; the launch traced here: 380 us
  blocking collectives  138 us (36%)
  other arithmetic  101 us (27%)
  local copies, waits for them, and re-layouts  87.7 us (23%)
  starting transfers between devices  42 us (11%)
  between operations  7.48 us (2%)
    psum x2, blocking collectives, per_device(): lax.psum((jnp.sum(residual * image), jnp.sum(image * image)), ('cells', '...  83.9 us
    scatter-add x4, other arithmetic, per_device(): jnp.zeros_like(flat).at[:, near_cells].add(flux_right).at[:, far_cells]  64.3 us
    psum x1, blocking collectives, squares(): return lax.psum(jnp.sum(residual * residual), ('cells', 'slab'))  42 us
    slice x2, local copies, waits for them, and re-layouts, per_device(): fault_term[0]  24.7 us
    ppermute x7, starting transfers between devices, shifted(): return lax.ppermute(value, axis, pairs)  21.4 us
    mul x4, other arithmetic, per_device(): scaled = mobile * precond  19.6 us
    gather x4, local copies, waits for them, and re-layouts, per_device(): picks_far = flat[:, far_cells]  19.3 us
    gather x4, local copies, waits for them, and re-layouts, per_device(): picks_near = flat[:, near_cells]  18.3 us
  transfers between devices with their start and end apart: 15, of which 0 were waited for; matrix products, arithmetic and copies ran while one was open for 20% of the time, Pallas kernels for 0%

commit v1 on v0

--- a/solution.py
+++ b/solution.py
@@ -2,6 +2,7 @@
 import jax.numpy as jnp
 from jax import lax
 from jax.sharding import PartitionSpec as P
+from jax.lax import psum
 
 WELLS = 16
 NSTEPS = 2
@@ -139,8 +140,9 @@
         )
         second = block[2] * precond[0] + block[3] * precond[1] + laplace[1] + fault_term[1]
         image = jnp.stack([first, second])
-        along, energy = lax.psum(
-            (jnp.sum(residual * image), jnp.sum(image * image)), ("cells", "slab")
+        wrap_sectors = lambda page, mesh_ax, device_axis: psum(psum(page, mesh_ax), device_axis)
+        along, energy = wrap_sectors(
+            (jnp.sum(residual * image), jnp.sum(image * image)), "slab", "cells"
         )
         history.append(jnp.sqrt(norm_square))
         alpha = along / energy

time: 381 us -> 347 us (0.911)
  blocking collectives: 138 us -> 107 us
    psum x2 -> x4, blocking collectives: 83.9 us -> 57.1 us  [the longest x2 41.6 us: per_device(): psum(psum(page, mesh_ax), device_axis)]
    psum x1, blocking collectives: 42 us -> 37.3 us  [squares(): return lax.psum(jnp.sum(residual * residual), ('cells', 'slab'))]
  transfers between devices with their start and end apart: 15 -> 15, of which waited for: 0 -> 0; matrix products, arithmetic and copies ran while one was open for 20% -> 22% of each run, Pallas kernels for 0% -> 0%
where the time goes in v1:
time: 347 us; the launch traced here: 345 us
  blocking collectives  107 us (31%)
  other arithmetic  101 us (29%)
  local copies, waits for them, and re-layouts  87.7 us (25%)
  starting transfers between devices  38.9 us (11%)
  between operations  7.48 us (2%)
    scatter-add x4, other arithmetic, per_device(): jnp.zeros_like(flat).at[:, near_cells].add(flux_right).at[:, far_cells]  64.3 us
    psum x2, blocking collectives, per_device(): psum(psum(page, mesh_ax), device_axis)  41.6 us
    psum x1, blocking collectives, squares(): return lax.psum(jnp.sum(residual * residual), ('cells', 'slab'))  37.3 us
    slice x2, local copies, waits for them, and re-layouts, per_device(): fault_term[0]  24.7 us
    ppermute x7, starting transfers between devices, shifted(): return lax.ppermute(value, axis, pairs)  21.4 us
    mul x4, other arithmetic, per_device(): scaled = mobile * precond  19.6 us
    gather x4, local copies, waits for them, and re-layouts, per_device(): picks_far = flat[:, far_cells]  19.3 us
    gather x4, local copies, waits for them, and re-layouts, per_device(): picks_near = flat[:, near_cells]  18.3 us
  transfers between devices with their start and end apart: 15, of which 0 were waited for; matrix products, arithmetic and copies ran while one was open for 22% of the time, Pallas kernels for 0%

profile of v1, /device:TPU:0, one launch (start us, length us, event | category | flops | bytes accessed | tf_op | source)
XLA Modules:
  0.0 344.9 jit_solution(14053276001658575606)
XLA Ops:
  0.6 0.9 broadcast_select_fusion.1
  1.7 4.9 %collective-permute-start = (f32[16]{0:T(128)S(1)}, f32[16]{0:T(128)S(1)}, u32[]{:S(2)}, u32[]{:S(2)}) collective-permute-start(f32[16]{0:T(128)S(1)} %slice_reduce_fusion.4), channel_id=1, source_target_pairs={{0,4},{4,8},{8,12},{12,16},{16,20},{20,24},{24,28},{1,5},{5,9},{9,... | collective-permute-start | bytes 200 | tf_op jit(solution)/shard_map/ppermute | solution.py:14
  6.6 0.9 broadcast_select_fusion
  7.5 1.5 collective-permute-start.1
  9.6 0.7 fusion.81
  10.3 3.4 collective-permute-start.7
  13.8 1.0 fusion.91
  14.7 0.7 compare_select_fusion
  15.5 0.7 compare_select_fusion.1
  16.2 0.7 and_select_fusion
  16.9 0.7 fusion.83
  17.6 1.0 multiply_add_fusion
  18.6 0.9 convolution_bitcast_fusion.3
  19.6 4.6 %copy.39 = f32[1,2,16,1024]{1,3,2,0:T(8,128)} copy(f32[1,2,16,1024]{3,2,1,0:T(8,128)S(1)} %get-tuple-element.39) | data formatting | bytes 262144 | tf_op jit(solution)/shard_map/slice | solution.py:88
  24.2 4.7 %copy.45 = f32[1,2,16,1024]{1,3,2,0:T(8,128)} copy(f32[1,2,16,1024]{3,2,1,0:T(8,128)S(1)} %get-tuple-element.38) | data formatting | bytes 262144 | tf_op jit(solution)/shard_map/slice | solution.py:88
  29.4 5.0 %copy.40 = f32[2,16384]{0,1:T(8,128)} copy(f32[2,16384]{1,0:T(2,128)S(1)} %pad_maximum_fusion.10) | data formatting | bytes 262144 | tf_op jit(solution)/shard_map/stack | solution.py:99
  34.4 9.8 %bitcast_multiply_fusion.1 = f32[2,16384]{0,1:T(8,128)} fusion(f32[2,16384]{0,1:T(8,128)} %copy.40, f32[1,2,16,1024]{1,3,2,0:T(8,128)} %copy.39), kind=kLoop, calls=%fused_computation.17 | loop fusion | flops 32768 | bytes 393216 | tf_op jit(solution)/shard_map/mul | solution.py:105
  44.2 8.8 %gather_fusion.1 = f32[2048,2]{1,0:T(8,128)S(1)} fusion(f32[2,16384]{0,1:T(8,128)} %bitcast_multiply_fusion.1, s32[2048]{0:T(1024)S(1)} %broadcast_clamp_fusion), kind=kCustom, calls=%fused_computation.1 | custom fusion | bytes 40960 | tf_op jit(solution)/shard_map/gather | solution.py:108
  53.4 1.3 collective-permute-start.6
  54.7 8.8 %gather_fusion = f32[2048,2]{1,0:T(8,128)S(1)} fusion(f32[2,16384]{0,1:T(8,128)} %bitcast_multiply_fusion.1, s32[2048]{0:T(1024)S(1)} %broadcast_clamp_fusion.1), kind=kCustom, calls=%fused_computation | custom fusion | bytes 40960 | tf_op jit(solution)/shard_map/gather | solution.py:107
  63.9 4.5 %collective-permute-start.8 = (f32[2,2048]{1,0:T(2,128)S(1)}, f32[2,2048]{1,0:T(2,128)S(1)}, u32[]{:S(2)}, u32[]{:S(2)}) collective-permute-start(f32[2,2048]{1,0:T(2,128)S(1)} %bitcast.381), channel_id=1, source_target_pairs={{0,4},{4,8},{8,12},{12,16},{16,20},{20,24},{24,28},{1,5},{5,9},{9,... | collective-permute-start | bytes 49160 | tf_op jit(solution)/shard_map/ppermute | solution.py:14
  68.5 1.3 collective-permute-start.2
  69.8 5.0 %collective-permute-start.3 = (f32[2,16,1]{2,1,0:T(8,128)S(1)}, f32[2,16,1]{2,1,0:T(8,128)S(1)}, u32[]{:S(2)}, u32[]{:S(2)}) collective-permute-start(f32[2,16,1]{2,1,0:T(8,128)S(1)} %get-tuple-element.47), channel_id=1, source_target_pairs={{0,4},{4,8},{8,12},{12,16},{16,20},{20,24},{24,28},{1,5},{5,9},{9,... | collective-permute-start | bytes 392 | tf_op jit(solution)/shard_map/ppermute | solution.py:22
  74.8 1.1 gather_fusion.2
  76.2 6.6 %all-reduce.5 = (f32[16]{0:T(128)S(1)}, f32[16]{0:T(128)S(1)}) all-reduce(f32[16]{0:T(128)S(1)} %convolution_bitcast_fusion.4, f32[16]{0:T(128)S(1)} %convolution_bitcast_fusion.3), channel_id=1, replica_groups=mesh['cells'=8,'slab'=4] {'slab'}, use_global_device_ids=true, to_apply=%region_2.3 | all-reduce | flops 32 | bytes 256 | tf_op jit(solution)/shard_map/psum | solution.py:130
  82.9 1.3 collective-permute-start.4
  84.2 3.0 collective-permute-start.5
  87.5 1.3 scatter_custom_fusion.2
  89.2 0.4 copy.43
  89.6 15.2 %scatter_custom_fusion = f32[2,16384]{0,1:T(8,128)} fusion(s32[2048]{0:T(1024)S(1)} %bitcast.386, f32[2048,2]{1,0:T(8,128)S(1)} %copy.43, f32[]{:T(128)} %constant.10.clone.1), kind=kCustom, calls=%fused_computation.20 | custom fusion | flops 4096 | bytes 131076 | tf_op jit(solution)/shard_map/scatter-add | solution.py:125
  104.8 0.4 copy.44
  105.1 16.9 %scatter_fusion = f32[2,16384]{0,1:T(8,128)} fusion(f32[2,16384]{0,1:T(8,128)} %scatter_custom_fusion, s32[2048]{0:T(1024)S(1)} %bitcast.376, f32[2048,2]{1,0:T(8,128)S(1)} %copy.44), kind=kCustom, calls=%fused_computation.7 | custom fusion | flops 4096 | bytes 57344 | tf_op jit(solution)/shard_map/scatter-add | solution.py:125
  122.0 12.5 %slice_reduce_fusion.3 = (f32[16384]{0:T(1024)S(1)}, f32[16384]{0:T(1024)S(1)}) fusion(f32[2,16384]{0,1:T(8,128)} %scatter_fusion), kind=kLoop, calls=%fused_computation.15 | loop fusion | bytes 262144 | tf_op jit(solution)/shard_map/slice | solution.py:139
  134.7 0.7 multiply_reduce_fusion.4
  135.3 7.5 %all-reduce.4 = (f32[]{:T(128)}, f32[]{:T(128)}) all-reduce(f32[]{:T(128)} %get-tuple-element.13, f32[]{:T(128)} %get-tuple-element.12), channel_id=1, replica_groups=mesh['cells'=8,'slab'=4] {'slab'}, use_global_device_ids=true, to_apply=%region_6.7 | all-reduce | flops 2 | bytes 16 | tf_op jit(solution)/shard_map/psum | solution.py:143
  142.9 20.6 %all-reduce.2 = (f32[]{:T(128)}, f32[]{:T(128)}) all-reduce(f32[]{:T(128)} %get-tuple-element.24, f32[]{:T(128)} %get-tuple-element.25), channel_id=1, replica_groups=mesh['cells'=8,'slab'=4] {'cells'}, use_global_device_ids=true, to_apply=%region_7.8 | all-reduce | flops 2 | bytes 16 | tf_op jit(solution)/shard_map/psum | solution.py:143
  165.2 5.0 %copy.46 = f32[2,16384]{0,1:T(8,128)} copy(f32[2,16384]{1,0:T(2,128)S(1)} %pad_maximum_fusion.12) | data formatting | bytes 262144 | tf_op jit(solution)/shard_map/stack | solution.py:99
  170.2 9.8 %bitcast_multiply_fusion = f32[2,16384]{0,1:T(8,128)} fusion(f32[2,16384]{0,1:T(8,128)} %copy.46, f32[1,2,16,1024]{1,3,2,0:T(8,128)} %copy.45), kind=kLoop, calls=%fused_computation.16 | loop fusion | flops 32768 | bytes 393216 | tf_op jit(solution)/shard_map/mul | solution.py:105
  180.0 8.8 %gather_fusion.3 = f32[2048,2]{1,0:T(8,128)S(1)} fusion(f32[2,16384]{0,1:T(8,128)} %bitcast_multiply_fusion, s32[2048]{0:T(1024)S(1)} %copy-done.13), kind=kCustom, calls=%fused_computation.3 | custom fusion | bytes 40960 | tf_op jit(solution)/shard_map/gather | solution.py:107
  188.9 9.8 %gather_fusion.4 = f32[2048,2]{1,0:T(8,128)S(1)} fusion(f32[2,16384]{0,1:T(8,128)} %bitcast_multiply_fusion, s32[2048]{0:T(1024)} %copy-done.11), kind=kCustom, calls=%fused_computation.4 | custom fusion | bytes 40960 | tf_op jit(solution)/shard_map/gather | solution.py:108
  198.7 1.5 fusion.31
  200.3 1.3 collective-permute-start.10
  201.6 1.3 collective-permute-start.9
  203.2 4.5 %collective-permute-start.14 = (f32[2,2048]{1,0:T(2,128)S(1)}, f32[2,2048]{1,0:T(2,128)S(1)}, u32[]{:S(2)}, u32[]{:S(2)}) collective-permute-start(f32[2,2048]{1,0:T(2,128)S(1)} %bitcast.382), channel_id=1, source_target_pairs={{0,4},{4,8},{8,12},{12,16},{16,20},{20,24},{24,28},{1,5},{5,9},{9,... | collective-permute-start | bytes 49160 | tf_op jit(solution)/shard_map/ppermute | solution.py:14
  208.1 1.3 collective-permute-start.13
  209.4 1.3 gather_fusion.5
  210.7 0.9 convolution_bitcast_fusion.1
  211.5 5.7 %psum.111 = f32[16]{0:T(128)S(1)} all-reduce(f32[16]{0:T(128)S(1)} %convolution_bitcast_fusion.1), channel_id=1, replica_groups=mesh['cells'=8,'slab'=4] {'slab'}, use_global_device_ids=true, to_apply=%region_13.14 | all-reduce | flops 16 | bytes 128 | tf_op jit(solution)/shard_map/psum | solution.py:130
  217.4 1.3 collective-permute-start.11
  218.7 3.0 collective-permute-start.12
  221.7 0.9 fusion.7
  222.6 1.5 scatter_custom_fusion.5
  224.1 1.8 fusion.10
  225.9 0.7 negate_bitcast_fusion
  227.4 15.3 %scatter_custom_fusion.3 = f32[2,16384]{0,1:T(8,128)} fusion(s32[2048]{0:T(1024)} %bitcast.387, f32[2048,2]{1,0:T(8,128)S(1)} %copy.49, f32[]{:T(128)} %constant.10.clone.1), kind=kCustom, calls=%fused_computation.18 | custom fusion | flops 4096 | bytes 131584 | tf_op jit(solution)/shard_map/scatter-add | solution.py:125
  242.7 16.9 %scatter_fusion.1 = f32[2,16384]{0,1:T(8,128)} fusion(f32[2,16384]{0,1:T(8,128)} %scatter_custom_fusion.3, s32[2048]{0:T(1024)S(1)} %bitcast.377, f32[2048,2]{1,0:T(8,128)S(1)} %copy.50), kind=kCustom, calls=%fused_computation.10 | custom fusion | flops 4096 | bytes 57344 | tf_op jit(solution)/shard_map/scatter-add | solution.py:125
  259.6 12.2 %slice_reduce_fusion.1 = (f32[16384]{0:T(1024)S(1)}, f32[16384]{0:T(1024)S(1)}) fusion(f32[2,16384]{0,1:T(8,128)} %scatter_fusion.1), kind=kLoop, calls=%fused_computation.13 | loop fusion | bytes 262144 | tf_op jit(solution)/shard_map/slice | solution.py:139
  271.9 0.6 multiply_reduce_fusion.2
  272.6 7.9 %all-reduce.3 = (f32[]{:T(128)}, f32[]{:T(128)}) all-reduce(f32[]{:T(128)} %get-tuple-element.11, f32[]{:T(128)} %get-tuple-element.10), channel_id=1, replica_groups=mesh['cells'=8,'slab'=4] {'slab'}, use_global_device_ids=true, to_apply=%region_16.17 | all-reduce | flops 2 | bytes 16 | tf_op jit(solution)/shard_map/psum | solution.py:143
  280.5 21.0 %all-reduce.1 = (f32[]{:T(128)}, f32[]{:T(128)}) all-reduce(f32[]{:T(128)} %get-tuple-element.22, f32[]{:T(128)} %get-tuple-element.23), channel_id=1, replica_groups=mesh['cells'=8,'slab'=4] {'cells'}, use_global_device_ids=true, to_apply=%region_17.18 | all-reduce | flops 2 | bytes 16 | tf_op jit(solution)/shard_map/psum | solution.py:143
  302.8 0.6 multiply_reduce_fusion.1
  303.5 37.3 %all-reduce = (f32[]{:T(128)}, f32[]{:T(128)}, f32[]{:T(128)}, f32[]{:T(128)}) all-reduce(f32[]{:T(128)} %get-tuple-element.9, f32[]{:T(128)} %get-tuple-element.8, f32[]{:T(128)} %get-tuple-element.7, f32[]{:T(128)} %get-tuple-element.6), channel_id=1, replica_groups=mesh['cells'=8,'slab'=4] {'cells','slab'}, use_global_device_ids=true, to_apply=%region_28.29 | all-reduce | flops 4 | bytes 32 | tf_op jit(solution)/shard_map/psum | solution.py:31
  343.6 0.6 pad_maximum_fusion.16
  344.2 0.7 pad_maximum_fusion
  (107 shorter events, 4.7 us)
Async XLA Ops:
  1.7 27.2 %collective-permute-start = (f32[16]{0:T(128)S(1)}, f32[16]{0:T(128)S(1)}, u32[]{:S(2)}, u32[]{:S(2)}) collective-permute-start(f32[16]{0:T(128)S(1)} %slice_reduce_fusion.4), channel_id=1, source_target_pairs={{0,4},{4,8},{8,12},{12,16},{16,20},{20,24},{24,28},{1,5},{5,9},{9,... | collective-permute-start | bytes 200 | tf_op jit(solution)/shard_map/ppermute | solution.py:14
  7.5 81.4 %copy-start.2 = (f32[16,1024]{1,0:T(8,128)}, f32[16,1024]{1,0:T(8,128)S(1)}, u32[]{:S(2)}) copy-start(f32[16,1024]{1,0:T(8,128)S(1)} %broadcast_select_fusion) | copy-start | bytes 196612
  7.5 21.4 %collective-permute-start.1 = (f32[1024]{0:T(1024)S(1)}, f32[1024]{0:T(1024)S(1)}, u32[]{:S(2)}, u32[]{:S(2)}) collective-permute-start(f32[1024]{0:T(1024)S(1)} %bitcast.389), channel_id=1, source_target_pairs={{0,1},{1,2},{2,3},{4,5},{5,6},{6,7},{8,9},{9,10},{10,11},{12,13},{... | collective-permute-start | bytes 12296 | tf_op jit(solution)/shard_map/ppermute | solution.py:14
  10.3 94.4 %collective-permute-start.7 = (f32[2048]{0:T(1024)S(1)}, f32[2048]{0:T(1024)S(1)}, u32[]{:S(2)}, u32[]{:S(2)}) collective-permute-start(f32[2048]{0:T(1024)S(1)} %fusion.81), channel_id=1, source_target_pairs={{0,4},{4,8},{8,12},{12,16},{16,20},{20,24},{24,28},{1,5},{5,9},{9,... | collective-permute-start | bytes 24584 | tf_op jit(solution)/shard_map/ppermute | solution.py:14
  15.5 28.7 %copy-start.11 = (s32[2048]{0:T(1024)}, s32[2048]{0:T(1024)S(1)}, u32[]{:S(2)}) copy-start(s32[2048]{0:T(1024)S(1)} %broadcast_clamp_fusion) | copy-start | bytes 24580
  16.2 73.4 %copy-start.15 = (s32[2048,1]{0,1:T(1,128)}, s32[2048,1]{0,1:T(1,128)S(1)}, u32[]{:S(2)}) copy-start(s32[2048,1]{0,1:T(1,128)S(1)} %compare_select_fusion.1) | copy-start | bytes 24580
  16.2 38.5 %copy-start.12 = (s32[2048]{0:T(1024)}, s32[2048]{0:T(1024)S(1)}, u32[]{:S(2)}) copy-start(s32[2048]{0:T(1024)S(1)} %broadcast_clamp_fusion.1) | copy-start | bytes 24580
  17.6 69.9 %copy-start.17 = (s32[128]{0:T(128)}, s32[128]{0:T(128)S(1)}, u32[]{:S(2)}) copy-start(s32[128]{0:T(128)S(1)} %fusion.83) | copy-start | bytes 1540
  19.5 55.3 %copy-start.16 = (s32[1024]{0:T(1024)}, s32[1024]{0:T(1024)S(1)}, u32[]{:S(2)}) copy-start(s32[1024]{0:T(1024)S(1)} %pad_clamp_fusion) | copy-start | bytes 12292
  19.5 9.4 %copy-start = (f32[2,4,16,1024]{3,2,1,0:T(8,128)S(1)}, f32[2,4,16,1024]{3,2,1,0:T(8,128)}, u32[]{:S(2)}) copy-start(f32[2,4,16,1024]{3,2,1,0:T(8,128)} %param.14) | copy-start | bytes 1572868
  19.5 9.4 %copy-start.1 = (f32[2,2,16,1024]{3,2,1,0:T(8,128)S(1)}, f32[2,2,16,1024]{3,2,1,0:T(8,128)}, u32[]{:S(2)}) copy-start(f32[2,2,16,1024]{3,2,1,0:T(8,128)} %param.15) | copy-start | bytes 786436
  19.5 9.4 %copy-start.9 = (f32[16,1024]{1,0:T(8,128)S(1)}, f32[16,1024]{1,0:T(8,128)}, u32[]{:S(2)}) copy-start(f32[16,1024]{1,0:T(8,128)} %param.17) | copy-start | bytes 196612
  19.5 9.4 %copy-start.10 = (f32[16,1024]{1,0:T(8,128)S(1)}, f32[16,1024]{1,0:T(8,128)}, u32[]{:S(2)}) copy-start(f32[16,1024]{1,0:T(8,128)} %param.18) | copy-start | bytes 196612
  29.1 59.8 %copy-start.3 = (f32[16,1024]{1,0:T(8,128)}, f32[16,1024]{1,0:T(8,128)S(1)}, u32[]{:S(2)}) copy-start(f32[16,1024]{1,0:T(8,128)S(1)} %get-tuple-element.30) | copy-start | bytes 196612
  29.1 59.8 %copy-start.4 = (f32[16,1024]{1,0:T(8,128)}, f32[16,1024]{1,0:T(8,128)S(1)}, u32[]{:S(2)}) copy-start(f32[16,1024]{1,0:T(8,128)S(1)} %get-tuple-element.31) | copy-start | bytes 196612
  34.4 41.6 %copy-start.18 = (s32[1,128]{1,0:T(1,128)S(1)}, s32[1,128]{1,0:T(1,128)}, u32[]{:S(2)}) copy-start(s32[1,128]{1,0:T(1,128)} %param.24) | copy-start | bytes 1540
  34.4 41.6 %copy-start.19 = (f32[1,128]{1,0:T(1,128)S(1)}, f32[1,128]{1,0:T(1,128)}, u32[]{:S(2)}) copy-start(f32[1,128]{1,0:T(1,128)} %param.25) | copy-start | bytes 1540
  53.4 35.8 %collective-permute-start.6 = (f32[2,2048]{1,0:T(2,128)S(1)}, f32[2,2048]{1,0:T(2,128)S(1)}, u32[]{:S(2)}, u32[]{:S(2)}) collective-permute-start(f32[2,2048]{1,0:T(2,128)S(1)} %bitcast.380), channel_id=1, source_target_pairs={{4,0},{8,4},{12,8},{16,12},{20,16},{24,20},{28,24},{5,1},{9,5},{13... | collective-permute-start | bytes 49160 | tf_op jit(solution)/shard_map/ppermute | solution.py:14
  63.9 40.9 %collective-permute-start.8 = (f32[2,2048]{1,0:T(2,128)S(1)}, f32[2,2048]{1,0:T(2,128)S(1)}, u32[]{:S(2)}, u32[]{:S(2)}) collective-permute-start(f32[2,2048]{1,0:T(2,128)S(1)} %bitcast.381), channel_id=1, source_target_pairs={{0,4},{4,8},{8,12},{12,16},{16,20},{20,24},{24,28},{1,5},{5,9},{9,... | collective-permute-start | bytes 49160 | tf_op jit(solution)/shard_map/ppermute | solution.py:14
  68.5 14.3 %collective-permute-start.2 = (f32[2,16,1]{2,1,0:T(8,128)S(1)}, f32[2,16,1]{2,1,0:T(8,128)S(1)}, u32[]{:S(2)}, u32[]{:S(2)}) collective-permute-start(f32[2,16,1]{2,1,0:T(8,128)S(1)} %get-tuple-element.46), channel_id=1, source_target_pairs={{4,0},{8,4},{12,8},{16,12},{20,16},{24,20},{28,24},{5,1},{9,5},{13... | collective-permute-start | bytes 392 | tf_op jit(solution)/shard_map/ppermute | solution.py:25
  69.8 13.0 %collective-permute-start.3 = (f32[2,16,1]{2,1,0:T(8,128)S(1)}, f32[2,16,1]{2,1,0:T(8,128)S(1)}, u32[]{:S(2)}, u32[]{:S(2)}) collective-permute-start(f32[2,16,1]{2,1,0:T(8,128)S(1)} %get-tuple-element.47), channel_id=1, source_target_pairs={{0,4},{4,8},{8,12},{12,16},{16,20},{20,24},{24,28},{1,5},{5,9},{9,... | collective-permute-start | bytes 392 | tf_op jit(solution)/shard_map/ppermute | solution.py:22
  82.8 4.5 %copy-start.20 = (f32[16]{0:T(128)}, f32[16]{0:T(128)S(1)}, u32[]{:S(2)}) copy-start(f32[16]{0:T(128)S(1)} %get-tuple-element.27) | copy-start | bytes 196
  82.9 5.9 %collective-permute-start.4 = (f32[2,1,1026]{2,1,0:T(1,128)S(1)}, f32[2,1,1026]{2,1,0:T(1,128)S(1)}, u32[]{:S(2)}, u32[]{:S(2)}) collective-permute-start(f32[2,1,1026]{2,1,0:T(1,128)S(1)} %get-tuple-element.42), channel_id=1, source_target_pairs={{1,0},{2,1},{3,2},{5,4},{6,5},{7,6},{9,8},{10,9},{11,10},{13,12},{... | collective-permute-start | bytes 24632 | tf_op jit(solution)/shard_map/ppermute | solution.py:25
  84.2 4.6 %collective-permute-start.5 = (f32[2,1,1026]{2,1,0:T(1,128)S(1)}, f32[2,1,1026]{2,1,0:T(1,128)S(1)}, u32[]{:S(2)}, u32[]{:S(2)}) collective-permute-start(f32[2,1,1026]{2,1,0:T(1,128)S(1)} %get-tuple-element.43), channel_id=1, source_target_pairs={{0,1},{1,2},{2,3},{4,5},{5,6},{6,7},{8,9},{9,10},{10,11},{12,13},{... | collective-permute-start | bytes 24632 | tf_op jit(solution)/shard_map/ppermute | solution.py:22
  104.7 29.8 %copy-start.14 = (f32[2048]{0:T(1024)}, f32[2048]{0:T(1024)S(1)}, u32[]{:S(2)}) copy-start(f32[2048]{0:T(1024)S(1)} %collective-permute-done.7) | copy-start | bytes 24580
  122.0 42.8 %copy-start.7 = (f32[2,2,16,1024]{3,2,1,0:T(8,128)S(1)}, f32[2,2,16,1024]{3,2,1,0:T(8,128)}, u32[]{:S(2)}) copy-start(f32[2,2,16,1024]{3,2,1,0:T(8,128)} %param.16) | copy-start | bytes 786436
  122.0 42.8 %copy-start.8 = (f32[2,2,16,1024]{3,2,1,0:T(8,128)S(1)}, f32[2,2,16,1024]{3,2,1,0:T(8,128)}, u32[]{:S(2)}) copy-start(f32[2,2,16,1024]{3,2,1,0:T(8,128)} %param.13) | copy-start | bytes 786436
  134.6 30.2 %copy-start.5 = (f32[1,16,1024]{2,1,0:T(8,128)}, f32[1,16,1024]{2,1,0:T(8,128)S(1)}, u32[]{:S(2)}) copy-start(f32[1,16,1024]{2,1,0:T(8,128)S(1)} %get-tuple-element.37) | copy-start | bytes 196612
  170.2 9.8 %copy-start.13 = (s32[2048]{0:T(1024)S(1)}, s32[2048]{0:T(1024)}, u32[]{:S(2)}) copy-start(s32[2048]{0:T(1024)} %copy-done.12) | copy-start | bytes 24580
  200.3 16.9 %collective-permute-start.10 = (f32[2,16,1]{2,1,0:T(8,128)S(1)}, f32[2,16,1]{2,1,0:T(8,128)S(1)}, u32[]{:S(2)}, u32[]{:S(2)}) collective-permute-start(f32[2,16,1]{2,1,0:T(8,128)S(1)} %get-tuple-element.45), channel_id=1, source_target_pairs={{0,4},{4,8},{8,12},{12,16},{16,20},{20,24},{24,28},{1,5},{5,9},{9,... | collective-permute-start | bytes 392 | tf_op jit(solution)/shard_map/ppermute | solution.py:22
  201.6 15.7 %collective-permute-start.9 = (f32[2,16,1]{2,1,0:T(8,128)S(1)}, f32[2,16,1]{2,1,0:T(8,128)S(1)}, u32[]{:S(2)}, u32[]{:S(2)}) collective-permute-start(f32[2,16,1]{2,1,0:T(8,128)S(1)} %get-tuple-element.44), channel_id=1, source_target_pairs={{4,0},{8,4},{12,8},{16,12},{20,16},{24,20},{28,24},{5,1},{9,5},{13... | collective-permute-start | bytes 392 | tf_op jit(solution)/shard_map/ppermute | solution.py:25
  203.2 22.7 %collective-permute-start.14 = (f32[2,2048]{1,0:T(2,128)S(1)}, f32[2,2048]{1,0:T(2,128)S(1)}, u32[]{:S(2)}, u32[]{:S(2)}) collective-permute-start(f32[2,2048]{1,0:T(2,128)S(1)} %bitcast.382), channel_id=1, source_target_pairs={{0,4},{4,8},{8,12},{12,16},{16,20},{20,24},{24,28},{1,5},{5,9},{9,... | collective-permute-start | bytes 49160 | tf_op jit(solution)/shard_map/ppermute | solution.py:14
  208.1 18.9 %collective-permute-start.13 = (f32[2,2048]{1,0:T(2,128)S(1)}, f32[2,2048]{1,0:T(2,128)S(1)}, u32[]{:S(2)}, u32[]{:S(2)}) collective-permute-start(f32[2,2048]{1,0:T(2,128)S(1)} %bitcast.383), channel_id=1, source_target_pairs={{4,0},{8,4},{12,8},{16,12},{20,16},{24,20},{28,24},{5,1},{9,5},{13... | collective-permute-start | bytes 49160 | tf_op jit(solution)/shard_map/ppermute | solution.py:14
  217.4 6.7 %collective-permute-start.11 = (f32[2,1,1026]{2,1,0:T(1,128)S(1)}, f32[2,1,1026]{2,1,0:T(1,128)S(1)}, u32[]{:S(2)}, u32[]{:S(2)}) collective-permute-start(f32[2,1,1026]{2,1,0:T(1,128)S(1)} %get-tuple-element.40), channel_id=1, source_target_pairs={{1,0},{2,1},{3,2},{5,4},{6,5},{7,6},{9,8},{10,9},{11,10},{13,12},{... | collective-permute-start | bytes 24632 | tf_op jit(solution)/shard_map/ppermute | solution.py:25
  218.7 5.4 %collective-permute-start.12 = (f32[2,1,1026]{2,1,0:T(1,128)S(1)}, f32[2,1,1026]{2,1,0:T(1,128)S(1)}, u32[]{:S(2)}, u32[]{:S(2)}) collective-permute-start(f32[2,1,1026]{2,1,0:T(1,128)S(1)} %get-tuple-element.41), channel_id=1, source_target_pairs={{0,1},{1,2},{2,3},{4,5},{5,6},{6,7},{8,9},{9,10},{10,11},{12,13},{... | collective-permute-start | bytes 24632 | tf_op jit(solution)/shard_map/ppermute | solution.py:22
  259.6 12.3 %copy-start.6 = (f32[2,16,1024]{2,1,0:T(8,128)S(1)}, f32[2,16,1024]{2,1,0:T(8,128)}, u32[]{:S(2)}) copy-start(f32[2,16,1024]{2,1,0:T(8,128)} %fusion.10) | copy-start | bytes 393220
